TPU v7x, 256 devices: a whole 4x4x8 slice. The times are simulated.
256 devices in a mesh: section: 4 (over y), expert: 64 (over x, z, core).
Axes of the slice: x: 4, y: 4, z: 8, core: 2. Of those that a mesh axis runs over, the one named last changes fastest.
Arguments:
- tokens: bfloat16 [1024, 4096], P('expert', 'section'), may hold values from -6 to 6
- cotangent: bfloat16 [1024, 4096], P('expert', 'section'), may hold values from -6 to 6
- routes: int32 [1024, 2], P('expert'), may hold values from 0 to 7, all different within a row; in each aligned block of 16 rows (0 to 15, 16 to 31, ...) at most 6 rows name the same one
- w_router: bfloat16 [4096, 8], P('section'), may hold values from -0.09375 to 0.09375
- w_gate: bfloat16 [64, 4096, 1024], P('expert', None, 'section'), may hold values from -0.09375 to 0.09375
- w_up: bfloat16 [64, 4096, 1024], P('expert', None, 'section'), may hold values from -0.09375 to 0.09375
- w_down: bfloat16 [64, 1024, 4096], P('expert', 'section'), may hold values from -0.0625 to 0.0625
Outputs:
- mixed: bfloat16 [1024, 4096], P('expert', 'section')
- grad_tokens: bfloat16 [1024, 4096], P('expert', 'section')
- grad_router: float32 [4096, 8], P('section')
- grad_gate: bfloat16 [64, 4096, 1024], P('expert', None, 'section')
- grad_up: bfloat16 [64, 4096, 1024], P('expert', None, 'section')
- grad_down: bfloat16 [64, 1024, 4096], P('expert', 'section')
Inputs may be any that keep to these rules, and one draw needn't show every extreme that they name: `routes`: each token names two different experts. Within each aligned block of 16 tokens no expert is named by more than 6 tokens, and in every draw some block has an expert named by exactly 6 tokens.
All inputs are finite; a program needn't handle non-finite values.
Results may differ from a plain program's by a relative error of at most 0.023.
Values may be sent and summed in bfloat16 or wider, within the bound.
No kernel may reach another device: no remote copies, remote signals or barrier semaphores. Data moves between devices by JAX's collectives and lax.ppermute only.
A program may use at most 128 MiB of HBM per device.

v0:
```python
import jax
import jax.numpy as jnp
import numpy as np
from jax import lax
from jax.sharding import Mesh
from jax.sharding import PartitionSpec as P

CAP = 6
LANES = 128
EXPERT_AXES = ("ex", "ez", "ec")


def expert_size():
    size = 1
    for name in EXPERT_AXES:
        size = size * lax.axis_size(name)
    return size


def per_device(tokens, cotangent, routes, w_router, w_gate, w_up, w_down):
    highest = lax.Precision.HIGHEST
    experts = w_router.shape[1]
    groups = expert_size() // experts
    capacity = CAP
    tok_count, width = tokens.shape
    n_section = lax.axis_size("section")
    slot_total = experts * capacity
    partial_logits = jnp.dot(tokens, w_router, preferred_element_type=jnp.float32)
    logits = lax.psum(partial_logits, "section")
    route_hot = routes[:, :, None] == jnp.arange(experts, dtype=jnp.int32)[None, None, :]
    zero_f = jnp.zeros((), jnp.float32)
    chosen = jnp.sum(jnp.where(route_hot, logits[:, None, :], zero_f), axis=2)
    gate_first = 1.0 / (1.0 + jnp.exp(chosen[:, 1] - chosen[:, 0]))
    gate_second = 1.0 / (1.0 + jnp.exp(chosen[:, 0] - chosen[:, 1]))
    counts_flat = route_hot.astype(jnp.int32).reshape(2 * tok_count, experts)
    earlier = jnp.cumsum(counts_flat, axis=0) - counts_flat
    position = jnp.sum(earlier * counts_flat, axis=1).reshape(tok_count, 2)
    slot_row = routes * capacity + position
    slot_ids = jnp.arange(slot_total, dtype=jnp.int32)[None, :]
    pick_first = slot_row[:, 0:1] == slot_ids
    pick_second = slot_row[:, 1:2] == slot_ids
    pick_both = (pick_first | pick_second).astype(jnp.bfloat16)
    x_source = jnp.einsum(
        "ts,td->sd", pick_both, tokens, preferred_element_type=jnp.float32
    ).astype(jnp.bfloat16)
    cot_float = cotangent.astype(jnp.float32)
    scaled_first = (gate_first[:, None] * cot_float).astype(jnp.bfloat16)
    scaled_second = (gate_second[:, None] * cot_float).astype(jnp.bfloat16)
    dy_source = jnp.einsum(
        "ts,td->sd",
        pick_first.astype(jnp.bfloat16),
        scaled_first,
        preferred_element_type=jnp.float32,
    )
    dy_source = dy_source + jnp.einsum(
        "ts,td->sd",
        pick_second.astype(jnp.bfloat16),
        scaled_second,
        preferred_element_type=jnp.float32,
    )
    dy_source = dy_source.astype(jnp.bfloat16)
    both_source = jnp.stack(
        [x_source.reshape(experts, capacity * width), dy_source.reshape(experts, capacity * width)],
        axis=1,
    )
    block_rows = 2 * capacity * width // LANES
    sent = jnp.broadcast_to(
        both_source.reshape(experts, 1, block_rows, LANES), (experts, groups, block_rows, LANES)
    ).reshape(experts * groups, block_rows, LANES)
    received = lax.all_to_all(sent, EXPERT_AXES, 0, 0, tiled=True)
    row_total = received.shape[0] * capacity
    received = received.reshape(-1, 2, capacity, width).transpose(1, 0, 2, 3)
    received = received.reshape(2, row_total, width)
    gathered = lax.all_gather(received, "section", axis=2, tiled=True)
    x_rows = gathered[0]
    dy_rows = gathered[1]
    gate_local = w_gate[0]
    up_local = w_up[0]
    down_local = w_down[0]
    pre_gate = jnp.dot(x_rows, gate_local, preferred_element_type=jnp.float32)
    pre_up = jnp.dot(x_rows, up_local, preferred_element_type=jnp.float32)
    sigmoid_gate = jax.nn.sigmoid(pre_gate)
    activated = pre_gate * sigmoid_gate
    hidden = (activated * pre_up).astype(jnp.bfloat16)
    d_hidden = jnp.einsum("pd,fd->pf", dy_rows, down_local, preferred_element_type=jnp.float32)
    grad_down = jnp.einsum("pf,pd->fd", hidden, dy_rows, preferred_element_type=jnp.float32).astype(
        jnp.bfloat16
    )
    d_pre_gate = (
        d_hidden * pre_up * sigmoid_gate * (1.0 + pre_gate * (1.0 - sigmoid_gate))
    ).astype(jnp.bfloat16)
    d_pre_up = (d_hidden * activated).astype(jnp.bfloat16)
    grad_gate = jnp.einsum(
        "pd,pf->df", x_rows, d_pre_gate, preferred_element_type=jnp.float32
    ).astype(jnp.bfloat16)
    grad_up = jnp.einsum("pd,pf->df", x_rows, d_pre_up, preferred_element_type=jnp.float32).astype(
        jnp.bfloat16
    )
    hid = gate_local.shape[1]
    down_blocks = down_local.reshape(hid, n_section, width)
    gate_blocks = gate_local.reshape(n_section, width, hid)
    up_blocks = up_local.reshape(n_section, width, hid)
    out_piece = jnp.einsum("pf,fsd->spd", hidden, down_blocks, preferred_element_type=jnp.float32)
    dx_piece = jnp.einsum(
        "pf,sdf->spd", d_pre_gate, gate_blocks, preferred_element_type=jnp.float32
    )
    dx_piece = dx_piece + jnp.einsum(
        "pf,sdf->spd", d_pre_up, up_blocks, preferred_element_type=jnp.float32
    )
    pieces = jnp.stack([out_piece, dx_piece], axis=1).astype(jnp.bfloat16)
    pieces = pieces.reshape(n_section * 2 * pieces.shape[2], width)
    reduced = lax.psum_scatter(pieces, "section", scatter_dimension=0, tiled=True)
    n_dev = row_total // capacity
    back = reduced.reshape(2, n_dev, capacity, width).transpose(1, 0, 2, 3)
    back = back.reshape(n_dev, block_rows, LANES)
    returned = lax.all_to_all(back, EXPERT_AXES, 0, 0, tiled=True)
    returned = returned.reshape(experts, groups, 2, capacity, width).astype(jnp.float32)
    folded = jnp.sum(returned, axis=1)
    slot_out = folded[:, 0].reshape(slot_total, width)
    slot_dx = folded[:, 1].reshape(slot_total, width)
    first_float = pick_first.astype(jnp.float32)
    second_float = pick_second.astype(jnp.float32)
    out_first = jnp.dot(first_float, slot_out, precision=highest)
    out_second = jnp.dot(second_float, slot_out, precision=highest)
    mixed = (gate_first[:, None] * out_first + gate_second[:, None] * out_second).astype(
        jnp.bfloat16
    )
    local_inner = jnp.stack(
        [jnp.sum(cot_float * out_first, axis=1), jnp.sum(cot_float * out_second, axis=1)], axis=1
    )
    gate_inner = lax.psum(local_inner, "section")
    d_first = gate_first * gate_second * (gate_inner[:, 0] - gate_inner[:, 1])
    d_logits = jnp.where(route_hot[:, 0, :], d_first[:, None], zero_f) - jnp.where(
        route_hot[:, 1, :], d_first[:, None], zero_f
    )
    dx_expert = jnp.dot(first_float, slot_dx, precision=highest)
    dx_expert = dx_expert + jnp.dot(second_float, slot_dx, precision=highest)
    router_float = w_router.astype(jnp.float32)
    grad_tokens = (dx_expert + jnp.dot(d_logits, router_float.T, precision=highest)).astype(
        jnp.bfloat16
    )
    router_part = jnp.einsum("te,tf->ef", d_logits, tokens.astype(jnp.float32), precision=highest)
    for name in reversed(EXPERT_AXES):
        router_part = lax.psum(router_part, name)
    grad_router = router_part.T
    return (mixed, grad_tokens, grad_router, grad_gate[None], grad_up[None], grad_down[None])


def expert_shape(devices):
    try:
        xs = sorted({d.coords[0] for d in devices.flat})
        zs = sorted({d.coords[2] for d in devices.flat})
        cores = sorted({d.core_on_chip for d in devices.flat})
        shape = (len(xs), len(zs), len(cores))
    except AttributeError:
        shape = (4, 8, 2)
    if int(np.prod(shape)) != devices.shape[1]:
        shape = (devices.shape[1] // 16, 8, 2)
    return shape


def solution(mesh):
    devices = mesh.devices
    fine = Mesh(
        devices.reshape((devices.shape[0],) + expert_shape(devices)), ("section",) + EXPERT_AXES
    )
    ex = EXPERT_AXES
    in_specs = (
        P(ex, "section"),
        P(ex, "section"),
        P(ex, None),
        P("section", None),
        P(ex, None, "section"),
        P(ex, None, "section"),
        P(ex, "section", None),
    )
    out_specs = (
        P(ex, "section"),
        P(ex, "section"),
        P("section", None),
        P(ex, None, "section"),
        P(ex, None, "section"),
        P(ex, "section", None),
    )
    return jax.shard_map(
        per_device, mesh=fine, in_specs=in_specs, out_specs=out_specs, check_vma=False
    )
```

profile of v0, /device:TPU:8, one launch (start us, length us, event | category | flops | bytes accessed | tf_op | source)
XLA Modules:
  0.0 387.1 jit_solution(12677243295857633148)
XLA Ops:
  7.2 0.0 copy-start
  7.2 0.0 all-gather.2.cloned.1.call-start
  7.2 1.0 fusion.58
  8.2 9.9 %psum.35 = f32[16,8]{0,1:T(8,128)S(1)} all-reduce(f32[16,8]{0,1:T(8,128)S(1)} %fusion.58), channel_id=1, replica_groups=mesh['section'=4,'ex'=4,'ez'=8,'ec'=2] {'section'}, use_global_device_ids=true, to_apply=%region_0.0 | all-reduce | flops 128 | bytes 1024 | tf_op jit(solution)/shard_map/psum | solution.py:29
  18.1 0.8 copy.44
  18.9 0.7 select_reduce_fusion.1
  19.6 0.1 eq.55
  19.7 0.1 fusion.35
  19.8 0.1 reduce_window_sum.11
  19.8 0.2 select_reduce_fusion
  20.0 0.1 reshape.42
  20.1 0.1 copy.45
  20.2 0.7 multiply_add_fusion
  20.9 1.0 convolution_convert_fusion.3
  21.9 0.1 stack_reshape.8
  22.0 1.0 fusion.31
  23.1 1.0 fusion.19
  24.1 0.1 stack_reshape.9
  24.2 0.5 pad_maximum_fusion.1
  24.6 0.1 broadcast_in_dim.58
  24.8 0.2 broadcast_in_dim.59
  25.0 50.1 %all_to_all.10 = bf16[64,96,128]{2,1,0:T(8,128)(2,1)} all-to-all(bf16[64,96,128]{2,1,0:T(8,128)(2,1)S(1)} %bitcast.103), channel_id=1, replica_groups=mesh['section'=4,'ex'=4,'ez'=8,'ec'=2] {'ex','ez','ec'}, dimensions={0} | all-to-all | bytes 3145728 | tf_op jit(solution)/shard_map/all_to_all | solution.py:70
  75.1 4.3 %reshape.44 = bf16[64,2,6,1024]{3,2,1,0:T(8,128)(2,1)} reshape(bf16[64,96,128]{2,1,0:T(8,128)(2,1)} %all_to_all.10) | data formatting | bytes 3145728 | tf_op jit(solution)/shard_map/reshape | solution.py:72
  79.5 4.4 %copy.48 = bf16[2,64,6,1024]{3,0,2,1:T(2,128)(2,1)} copy(bf16[2,64,6,1024]{3,2,0,1:T(8,128)(2,1)} %bitcast.100) | data formatting | bytes 3145728 | tf_op jit(solution)/shard_map/transpose | solution.py:72
  83.8 0.0 all-gather.2.cloned.1.call-update
  83.8 0.0 reduce-scatter.2.cloned.1.call-start
  83.9 4.5 %reshape_squeeze.15 = bf16[256,4,1024]{2,1,0:T(4,128)(2,1)} reshape(bf16[1,256,4096]{2,1,0:T(8,128)(2,1)} %param.13) | data formatting | bytes 4194304 | tf_op jit(solution)/shard_map/reshape;squeeze | solution.py:100
  88.4 63.9 %all-gather.2.cloned.1.call-done = bf16[2,384,4096]{2,0,1:T(2,128)(2,1)} async-done(((bf16[2,384,1024]{2,0,1:T(2,128)(2,1)}), bf16[2,384,4096]{2,0,1:T(2,128)(2,1)}) %all-gather.2.cloned.1.call-update) | async-done | bytes 6291472 | tf_op jit(solution)/shard_map/all_gather | solution.py:74
  152.3 15.7 %fusion.56 = (bf16[1,384,4096]{2,0,1:T(2,128)(2,1)S(1)}, bf16[1,384,4096]{2,0,1:T(2,128)(2,1)S(1)}) fusion(bf16[2,384,4096]{2,0,1:T(2,128)(2,1)} %all-gather.2.cloned.1.call-done), kind=kLoop, calls=%fused_computation.89 | loop fusion | bytes 12582912 | tf_op jit(solution)/shard_map/slice | solution.py:76
  168.0 0.0 copy-start.6
  168.0 3.7 copy.52
  171.7 0.0 copy-start.7
  171.7 3.6 fusion.5
  175.4 1.0 fusion.11
  176.4 0.0 copy-start.3
  176.4 1.1 multiply_convert_fusion.2
  177.5 0.5 copy-done.3
  178.0 1.7 convert_bitcast_fusion
  179.7 1.0 fusion.23
  180.7 1.4 fusion.3
  182.1 0.6 pad_maximum_fusion
  182.7 3.4 copy.50
  186.1 0.0 reduce-scatter.2.cloned.1.call-update
  186.1 67.1 %reduce-scatter.2.cloned.1.call-done = bf16[768,1024]{1,0:T(8,128)(2,1)} async-done(((bf16[3072,1024]{1,0:T(8,128)(2,1)}), bf16[768,1024]{1,0:T(8,128)(2,1)}) %reduce-scatter.2.cloned.1.call-update) | async-done | bytes 1572880 | tf_op jit(solution)/shard_map/reduce_scatter | solution.py:112
  253.2 2.5 reshape.46
  255.7 1.6 copy.51
  257.3 4.4 %reshape.47 = bf16[64,96,128]{2,1,0:T(8,128)(2,1)} reshape(bf16[64,2,6,1024]{3,2,1,0:T(8,128)(2,1)} %copy.51) | data formatting | bytes 3145728 | tf_op jit(solution)/shard_map/reshape | solution.py:115
  261.7 10.7 %all-to-all-start.1 = ((bf16[64,96,128]{2,1,0:T(8,128)(2,1)}), bf16[64,96,128]{2,1,0:T(8,128)(2,1)}, u32[]{:S(2)}, u32[]{:S(2)}) async-start(bf16[64,96,128]{2,1,0:T(8,128)(2,1)} %reshape.47), calls=%async_computation.2 | async-start | bytes 3145728 | tf_op jit(solution)/shard_map/all_to_all | solution.py:116
  272.4 8.2 %fusion.2 = bf16[1,256,4096]{2,1,0:T(8,128)(2,1)} fusion(bf16[384,256]{1,0:T(8,128)(2,1)S(1)} %get-tuple-element.10, bf16[1,384,4096]{2,0,1:T(2,128)(2,1)} %copy-done.2), kind=kOutput, calls=%fused_computation.7 | convolution fusion | flops 806354944 | bytes 5439488 | tf_op jit(solution)/shard_map/pf,pd->fd/dot_general | solution.py:86
  280.6 2.6 fusion
  283.2 2.6 fusion.1
  285.8 25.9 %all-to-all-done.1 = bf16[64,96,128]{2,1,0:T(8,128)(2,1)} async-done(((bf16[64,96,128]{2,1,0:T(8,128)(2,1)}), bf16[64,96,128]{2,1,0:T(8,128)(2,1)}, u32[]{:S(2)}, u32[]{:S(2)}) %all-to-all-start.1) | async-done | bytes 1572896 | tf_op jit(solution)/shard_map/all_to_all | solution.py:116
  311.7 4.7 %reshape.48 = f32[8,8,2,6,1024]{4,3,2,1,0:T(8,128)} reshape(bf16[64,96,128]{2,1,0:T(8,128)(2,1)} %all-to-all-done.1) | data formatting | bytes 4718592 | tf_op jit(solution)/shard_map/convert_element_type | solution.py:117
  316.4 2.7 reduce_sum.47
  319.2 0.2 fusion.38
  319.5 0.2 convolution_add_fusion.2
  319.7 0.2 fusion.36
  320.0 1.0 fusion.28
  321.0 9.5 %psum.36 = f32[16,2]{0,1:T(2,128)S(1)} all-reduce(f32[16,2]{0,1:T(2,128)S(1)} %pad_maximum_fusion.2), channel_id=1, replica_groups=mesh['section'=4,'ex'=4,'ez'=8,'ec'=2] {'section'}, use_global_device_ids=true, to_apply=%region_8.9 | all-reduce | flops 32 | bytes 256 | tf_op jit(solution)/shard_map/psum | solution.py:131
  330.5 0.1 fusion.41
  330.6 0.8 fusion.20
  331.5 3.4 psum.37
  334.9 28.5 %psum.38 = f32[8,1024]{1,0:T(8,128)S(1)} all-reduce(f32[8,1024]{1,0:T(8,128)S(1)} %psum.37), channel_id=1, replica_groups=mesh['section'=4,'ex'=4,'ez'=8,'ec'=2] {'ez'}, use_global_device_ids=true, to_apply=%region_10.11 | all-reduce | flops 8192 | bytes 65536 | tf_op jit(solution)/shard_map/psum | solution.py:144
  363.3 16.9 %psum.39 = f32[1024,8]{0,1:T(8,128)} all-reduce(f32[1024,8]{0,1:T(8,128)S(1)} %bitcast.105), channel_id=1, replica_groups=mesh['section'=4,'ex'=4,'ez'=8,'ec'=2] {'ex'}, use_global_device_ids=true, to_apply=%region_11.12 | all-reduce | flops 8192 | bytes 65536 | tf_op jit(solution)/shard_map/psum | solution.py:144
  (27 shorter events, 0.2 us)
Async XLA Ops:
  7.2 169.2 %copy-start = (bf16[1,4096,256]{2,1,0:T(8,128)(2,1)S(1)}, bf16[1,4096,256]{2,1,0:T(8,128)(2,1)}, u32[]{:S(2)}) copy-start(bf16[1,4096,256]{2,1,0:T(8,128)(2,1)} %param.12) | copy-start | bytes 6291460
  7.2 145.1 %all-gather.2.cloned.1.call-start = ((), (), s32[]{:S(2)}) async-start(), calls=%async_computation.3 | async-start | bytes 7864320 | tf_op jit(solution)/shard_map/all_gather | solution.py:74
  83.8 169.4 %reduce-scatter.2.cloned.1.call-start = ((), (), s32[]{:S(2)}) async-start(), calls=%async_computation.4 | async-start | bytes 7864320 | tf_op jit(solution)/shard_map/reduce_scatter | solution.py:112
  168.0 3.7 copy-start.2
  168.0 3.7 copy-start.6
  171.7 4.7 %copy-start.4 = (bf16[1,384,4096]{2,1,0:T(8,128)(2,1)}, bf16[1,384,4096]{2,1,0:T(8,128)(2,1)S(1)}, u32[]{:S(2)}) copy-start(bf16[1,384,4096]{2,1,0:T(8,128)(2,1)S(1)} %copy.52) | copy-start | bytes 9437188
  171.7 3.6 copy-start.7
  176.4 1.6 copy-start.3
  257.3 15.1 %copy-start.11 = (s32[16,2]{0,1:T(2,128)S(1)}, s32[16,2]{0,1:T(2,128)}, u32[]{:S(2)}) copy-start(s32[16,2]{0,1:T(2,128)} %param.9) | copy-start | bytes 388
  261.7 50.0 %all-to-all-start.1 = ((bf16[64,96,128]{2,1,0:T(8,128)(2,1)}), bf16[64,96,128]{2,1,0:T(8,128)(2,1)}, u32[]{:S(2)}, u32[]{:S(2)}) async-start(bf16[64,96,128]{2,1,0:T(8,128)(2,1)} %reshape.47), calls=%async_computation.2 | async-start | bytes 3145728 | tf_op jit(solution)/shard_map/all_to_all | solution.py:116
  272.3 8.3 %copy-start.5 = (bf16[1,384,4096]{2,1,0:T(8,128)(2,1)S(1)}, bf16[1,384,4096]{2,1,0:T(8,128)(2,1)}, u32[]{:S(2)}) copy-start(bf16[1,384,4096]{2,1,0:T(8,128)(2,1)} %copy-done.4) | copy-start | bytes 9437188
  311.7 68.5 %copy-start.1 = (bf16[1,4096,256]{2,1,0:T(8,128)(2,1)S(1)}, bf16[1,4096,256]{2,1,0:T(8,128)(2,1)}, u32[]{:S(2)}) copy-start(bf16[1,4096,256]{2,1,0:T(8,128)(2,1)} %param.12) | copy-start | bytes 6291460
  316.4 3.6 copy-start.8
  316.4 14.1 %copy-start.9 = (bf16[16,1024]{1,0:T(8,128)(2,1)S(1)}, bf16[16,1024]{1,0:T(8,128)(2,1)}, u32[]{:S(2)}) copy-start(bf16[16,1024]{1,0:T(8,128)(2,1)} %param.7) | copy-start | bytes 98308
  316.4 14.2 %copy-start.10 = (bf16[1024,8]{0,1:T(8,128)(2,1)S(1)}, bf16[1024,8]{0,1:T(8,128)(2,1)}, u32[]{:S(2)}) copy-start(bf16[1024,8]{0,1:T(8,128)(2,1)} %param.10) | copy-start | bytes 49156
Sparse Core Ops, SparseCore 0:
  84.0 68.2 all-gather.1
  186.2 66.9 reduce-scatter.1
where the time goes:
time: 388 us; the launch traced here: 387 us
  waiting for transfers between devices  157 us (40%)
  blocking collectives  118 us (30%)
  local copies, waits for them, and re-layouts  51.2 us (13%)
  matrix products  30 us (8%)
  between operations  14.4 us (4%)
  starting transfers between devices  10.7 us (3%)
  other arithmetic  5.51 us (1%)
    reduce_scatter x1, waiting for transfers between devices, per_device(): lax.psum_scatter(pieces, 'section', scatter_dimension=0, tiled=True)  67.1 us
    all_gather x1, waiting for transfers between devices, per_device(): gathered = lax.all_gather(received, 'section', axis=2, tiled=True)  63.9 us
    all_to_all x1, blocking collectives, per_device(): received = lax.all_to_all(sent, EXPERT_AXES, 0, 0, tiled=True)  50.1 us
    psum x3, blocking collectives, per_device(): router_part = lax.psum(router_part, name)  48.7 us
    all_to_all x1, waiting for transfers between devices, per_device(): returned = lax.all_to_all(back, EXPERT_AXES, 0, 0, tiled=True)  25.9 us
    slice x1, local copies, waits for them, and re-layouts, per_device(): dy_rows = gathered[1]  15.7 us
    all_to_all x1, starting transfers between devices, per_device(): returned = lax.all_to_all(back, EXPERT_AXES, 0, 0, tiled=True)  10.7 us
    psum x1, blocking collectives, per_device(): logits = lax.psum(partial_logits, 'section')  9.88 us
  transfers between devices with their start and end apart: 3, of which 3 were waited for; matrix products, arithmetic and copies ran while one was open for 5% of the time, Pallas kernels for 0%

commit v1 on v0

--- a/solution.py
+++ b/solution.py
@@ -71,7 +71,9 @@
     row_total = received.shape[0] * capacity
     received = received.reshape(-1, 2, capacity, width).transpose(1, 0, 2, 3)
     received = received.reshape(2, row_total, width)
-    gathered = lax.all_gather(received, "section", axis=2, tiled=True)
+    gathered = jnp.concatenate(
+        lax.all_to_all(jnp.stack([received] * lax.axis_size("section")), "section", 0, 0), axis=2
+    )
     x_rows = gathered[0]
     dy_rows = gathered[1]
     gate_local = w_gate[0]

time: 388 us -> 386 us (level)
  starting transfers between devices: 10.7 us -> 18.6 us
  matrix products: 30 us -> 23.6 us
    all_to_all x0 -> x1, waiting for transfers between devices: none -> 66.2 us  [per_device(): lax.all_to_all(jnp.stack([received] * lax.axis_size('section')), 'section...]
    all_gather x1 -> x0, waiting for transfers between devices: 63.9 us -> none  [per_device(): gathered = lax.all_gather(received, 'section', axis=2, tiled=True)]
    slice x1, local copies, waits for them, and re-layouts: 15.7 us -> 0.66 us  [per_device(): dy_rows = gathered[1]]
    another operation x0 -> x2, local copies, waits for them, and re-layouts: none -> 9.52 us  [per_device(): jnp.stack([received] * lax.axis_size('section'))]
    all_to_all x0 -> x1, starting transfers between devices: none -> 7.69 us  [per_device(): lax.all_to_all(jnp.stack([received] * lax.axis_size('section')), 'section...]
    reduce_scatter x1, waiting for transfers between devices: 67.1 us -> 61.3 us  [per_device(): lax.psum_scatter(pieces, 'section', scatter_dimension=0, tiled=True)]
  transfers between devices with their start and end apart: 3 -> 3, of which waited for: 3 -> 3; matrix products, arithmetic and copies ran while one was open for 5% -> 4% of each run, Pallas kernels for 0% -> 0%
where the time goes in v1:
time: 386 us; the launch traced here: 385 us
  waiting for transfers between devices  157 us (41%)
  blocking collectives  118 us (31%)
  local copies, waits for them, and re-layouts  47.7 us (12%)
  matrix products  23.6 us (6%)
  starting transfers between devices  18.6 us (5%)
  between operations  14.3 us (4%)
  other arithmetic  5.51 us (1%)
    all_to_all x1, waiting for transfers between devices, per_device(): lax.all_to_all(jnp.stack([received] * lax.axis_size('section')), 'section...  66.2 us
    reduce_scatter x1, waiting for transfers between devices, per_device(): lax.psum_scatter(pieces, 'section', scatter_dimension=0, tiled=True)  61.3 us
    all_to_all x1, blocking collectives, per_device(): received = lax.all_to_all(sent, EXPERT_AXES, 0, 0, tiled=True)  50.1 us
    psum x3, blocking collectives, per_device(): router_part = lax.psum(router_part, name)  48.7 us
    all_to_all x1, waiting for transfers between devices, per_device(): returned = lax.all_to_all(back, EXPERT_AXES, 0, 0, tiled=True)  29.3 us
    all_to_all x1, starting transfers between devices, per_device(): returned = lax.all_to_all(back, EXPERT_AXES, 0, 0, tiled=True)  10.9 us
    psum x1, blocking collectives, per_device(): logits = lax.psum(partial_logits, 'section')  9.88 us
    another operation x2, local copies, waits for them, and re-layouts, per_device(): jnp.stack([received] * lax.axis_size('section'))  9.52 us
  transfers between devices with their start and end apart: 3, of which 3 were waited for; matrix products, arithmetic and copies ran while one was open for 4% of the time, Pallas kernels for 0%

profile of v1, /device:TPU:8, one launch (start us, length us, event | category | flops | bytes accessed | tf_op | source)
XLA Modules:
  0.0 384.9 jit_solution(4120969256749700925)
XLA Ops:
  7.2 0.0 copy-start
  7.2 1.0 fusion.50
  8.2 9.9 %psum.35 = f32[16,8]{0,1:T(8,128)S(1)} all-reduce(f32[16,8]{0,1:T(8,128)S(1)} %fusion.50), channel_id=1, replica_groups=mesh['section'=4,'ex'=4,'ez'=8,'ec'=2] {'section'}, use_global_device_ids=true, to_apply=%region_0.0 | all-reduce | flops 128 | bytes 1024 | tf_op jit(solution)/shard_map/psum | solution.py:29
  18.1 0.8 copy.38
  18.9 0.7 select_reduce_fusion.1
  19.6 0.1 eq.55
  19.7 0.1 fusion.27
  19.7 0.1 reduce_window_sum.11
  19.8 0.2 select_reduce_fusion
  20.0 0.1 reshape.49
  20.1 0.1 copy.39
  20.1 0.7 multiply_add_fusion
  20.9 1.0 convolution_convert_fusion.3
  21.9 0.1 stack_reshape.15
  22.0 1.0 fusion.23
  23.0 1.0 fusion.11
  24.1 0.1 stack_reshape.16
  24.2 0.5 pad_maximum_fusion.1
  24.6 0.1 broadcast_in_dim.58
  24.7 0.2 broadcast_in_dim.59
  25.0 50.1 %all_to_all.15 = bf16[64,96,128]{2,1,0:T(8,128)(2,1)} all-to-all(bf16[64,96,128]{2,1,0:T(8,128)(2,1)S(1)} %bitcast.104), channel_id=1, replica_groups=mesh['section'=4,'ex'=4,'ez'=8,'ec'=2] {'ex','ez','ec'}, dimensions={0} | all-to-all | bytes 3145728 | tf_op jit(solution)/shard_map/all_to_all | solution.py:70
  75.1 4.3 %reshape.51 = bf16[64,2,6,1024]{3,2,1,0:T(8,128)(2,1)} reshape(bf16[64,96,128]{2,1,0:T(8,128)(2,1)} %all_to_all.15) | data formatting | bytes 3145728 | tf_op jit(solution)/shard_map/reshape | solution.py:72
  79.4 4.4 %copy.42 = bf16[2,64,6,1024]{3,0,2,1:T(2,128)(2,1)} copy(bf16[2,64,6,1024]{3,2,0,1:T(8,128)(2,1)} %bitcast.102) | data formatting | bytes 3145728 | tf_op jit(solution)/shard_map/transpose | solution.py:72
  83.8 4.9 %copy.43 = bf16[2,384,1024]{1,2,0:T(8,128)(2,1)} copy(bf16[2,384,1024]{2,0,1:T(2,128)(2,1)} %bitcast.105) | data formatting | bytes 3145728 | tf_op jit(solution)/shard_map/stack;reshape | solution.py:75
  88.7 4.6 %stack.28 = bf16[4,2,384,1024]{2,3,1,0:T(8,128)(2,1)} broadcast(bf16[2,384,1024]{1,2,0:T(8,128)(2,1)} %copy.43), dimensions={1,2,3} | broadcast | bytes 7864320 | tf_op jit(solution)/shard_map/stack | solution.py:75
  93.3 7.7 %all-to-all-start.1 = ((bf16[4,2,384,1024]{2,3,1,0:T(8,128)(2,1)}), bf16[4,2,384,1024]{2,3,1,0:T(8,128)(2,1)}, u32[]{:S(2)}, u32[]{:S(2)}) async-start(bf16[4,2,384,1024]{2,3,1,0:T(8,128)(2,1)} %stack.28), calls=%async_computation.1 | async-start | bytes 12582912 | tf_op jit(solution)/shard_map/all_to_all | solution.py:75
  101.0 4.5 %reshape_squeeze.15 = bf16[256,4,1024]{2,1,0:T(4,128)(2,1)} reshape(bf16[1,256,4096]{2,1,0:T(8,128)(2,1)} %param.13) | data formatting | bytes 4194304 | tf_op jit(solution)/shard_map/reshape;squeeze | solution.py:102
  105.5 66.2 %all-to-all-done.1 = bf16[4,2,384,1024]{2,3,1,0:T(8,128)(2,1)} async-done(((bf16[4,2,384,1024]{2,3,1,0:T(8,128)(2,1)}), bf16[4,2,384,1024]{2,3,1,0:T(8,128)(2,1)}, u32[]{:S(2)}, u32[]{:S(2)}) %all-to-all-start.1) | async-done | bytes 6291488 | tf_op jit(solution)/shard_map/all_to_all | solution.py:75
  171.7 3.4 copy.51
  175.1 0.0 copy-start.6
  175.2 0.7 fusion.48
  175.9 0.9 copy-done.6
  176.7 1.1 fusion.4
  177.8 1.4 copy-done.7
  179.2 1.1 fusion.8
  180.3 1.1 multiply_convert_fusion.2
  181.4 0.5 copy-done.5
  181.9 1.7 convert_bitcast_fusion
  183.6 1.0 fusion.15
  184.6 1.2 fusion.3
  185.8 0.6 pad_maximum_fusion
  186.3 3.4 copy.46
  189.7 0.0 reduce-scatter.2.cloned.1.call-update
  189.7 61.3 %reduce-scatter.2.cloned.1.call-done = bf16[768,1024]{1,0:T(8,128)(2,1)} async-done(((bf16[3072,1024]{1,0:T(8,128)(2,1)}), bf16[768,1024]{1,0:T(8,128)(2,1)}) %reduce-scatter.2.cloned.1.call-update) | async-done | bytes 1572880 | tf_op jit(solution)/shard_map/reduce_scatter | solution.py:114
  251.0 2.5 reshape.53
  253.5 1.6 copy.47
  255.1 4.4 %reshape.54 = bf16[64,96,128]{2,1,0:T(8,128)(2,1)} reshape(bf16[64,2,6,1024]{3,2,1,0:T(8,128)(2,1)} %copy.47) | data formatting | bytes 3145728 | tf_op jit(solution)/shard_map/reshape | solution.py:117
  259.4 10.9 %all-to-all-start.2 = ((bf16[64,96,128]{2,1,0:T(8,128)(2,1)}), bf16[64,96,128]{2,1,0:T(8,128)(2,1)}, u32[]{:S(2)}, u32[]{:S(2)}) async-start(bf16[64,96,128]{2,1,0:T(8,128)(2,1)} %reshape.54), calls=%async_computation.3 | async-start | bytes 3145728 | tf_op jit(solution)/shard_map/all_to_all | solution.py:118
  270.4 4.7 %fusion.2 = bf16[1,256,4096]{2,1,0:T(8,128)(2,1)} fusion(bf16[384,256]{1,0:T(8,128)(2,1)S(1)} %get-tuple-element.10, bf16[384,4096]{0,1:T(8,128)(2,1)} %bitcast.101), kind=kOutput, calls=%fused_computation.8 | convolution fusion | flops 806354944 | bytes 5439488 | tf_op jit(solution)/shard_map/pf,pd->fd/dot_general | solution.py:88
  275.0 2.6 fusion
  277.6 2.6 fusion.1
  280.2 29.3 %all-to-all-done.2 = bf16[64,96,128]{2,1,0:T(8,128)(2,1)} async-done(((bf16[64,96,128]{2,1,0:T(8,128)(2,1)}), bf16[64,96,128]{2,1,0:T(8,128)(2,1)}, u32[]{:S(2)}, u32[]{:S(2)}) %all-to-all-start.2) | async-done | bytes 1572896 | tf_op jit(solution)/shard_map/all_to_all | solution.py:118
  309.5 4.7 %reshape.55 = f32[8,8,2,6,1024]{4,3,2,1,0:T(8,128)} reshape(bf16[64,96,128]{2,1,0:T(8,128)(2,1)} %all-to-all-done.2) | data formatting | bytes 4718592 | tf_op jit(solution)/shard_map/convert_element_type | solution.py:119
  314.2 2.7 reduce_sum.47
  317.0 0.2 fusion.30
  317.3 0.2 convolution_add_fusion.2
  317.6 0.2 fusion.28
  317.8 1.0 fusion.20
  318.8 9.5 %psum.36 = f32[16,2]{0,1:T(2,128)S(1)} all-reduce(f32[16,2]{0,1:T(2,128)S(1)} %pad_maximum_fusion.2), channel_id=1, replica_groups=mesh['section'=4,'ex'=4,'ez'=8,'ec'=2] {'section'}, use_global_device_ids=true, to_apply=%region_8.9 | all-reduce | flops 32 | bytes 256 | tf_op jit(solution)/shard_map/psum | solution.py:133
  328.3 0.1 fusion.33
  328.4 0.8 fusion.12
  329.3 3.4 psum.37
  332.7 28.5 %psum.38 = f32[8,1024]{1,0:T(8,128)S(1)} all-reduce(f32[8,1024]{1,0:T(8,128)S(1)} %psum.37), channel_id=1, replica_groups=mesh['section'=4,'ex'=4,'ez'=8,'ec'=2] {'ez'}, use_global_device_ids=true, to_apply=%region_10.11 | all-reduce | flops 8192 | bytes 65536 | tf_op jit(solution)/shard_map/psum | solution.py:146
  361.2 16.9 %psum.39 = f32[1024,8]{0,1:T(8,128)} all-reduce(f32[1024,8]{0,1:T(8,128)S(1)} %bitcast.107), channel_id=1, replica_groups=mesh['section'=4,'ex'=4,'ez'=8,'ec'=2] {'ex'}, use_global_device_ids=true, to_apply=%region_11.12 | all-reduce | flops 8192 | bytes 65536 | tf_op jit(solution)/shard_map/psum | solution.py:146
  (28 shorter events, 0.2 us)
Async XLA Ops:
  7.2 173.1 %copy-start = (bf16[1,4096,256]{2,1,0:T(8,128)(2,1)S(1)}, bf16[1,4096,256]{2,1,0:T(8,128)(2,1)}, u32[]{:S(2)}) copy-start(bf16[1,4096,256]{2,1,0:T(8,128)(2,1)} %param.12) | copy-start | bytes 6291460
  93.3 78.4 %all-to-all-start.1 = ((bf16[4,2,384,1024]{2,3,1,0:T(8,128)(2,1)}), bf16[4,2,384,1024]{2,3,1,0:T(8,128)(2,1)}, u32[]{:S(2)}, u32[]{:S(2)}) async-start(bf16[4,2,384,1024]{2,3,1,0:T(8,128)(2,1)} %stack.28), calls=%async_computation.1 | async-start | bytes 12582912 | tf_op jit(solution)/shard_map/all_to_all | solution.py:75
  101.0 150.0 %reduce-scatter.2.cloned.1.call-start = ((), (), s32[]{:S(2)}) async-start(), calls=%async_computation.4 | async-start | bytes 7864320 | tf_op jit(solution)/shard_map/reduce_scatter | solution.py:114
  175.1 1.6 copy-start.6
  175.8 4.4 %copy-start.2 = (bf16[1,384,4,1024]{1,3,2,0:T(8,128)(2,1)}, bf16[1,384,4,1024]{1,3,2,0:T(8,128)(2,1)S(1)}, u32[]{:S(2)}) copy-start(bf16[1,384,4,1024]{1,3,2,0:T(8,128)(2,1)S(1)} %get-tuple-element.9) | copy-start | bytes 9437188
  175.8 4.4 %copy-start.4 = (bf16[1,384,4,1024]{1,3,2,0:T(8,128)(2,1)}, bf16[1,384,4,1024]{1,3,2,0:T(8,128)(2,1)S(1)}, u32[]{:S(2)}) copy-start(bf16[1,384,4,1024]{1,3,2,0:T(8,128)(2,1)S(1)} %get-tuple-element.8) | copy-start | bytes 9437188
  175.8 3.3 copy-start.7
  180.3 1.6 copy-start.5
  255.1 15.3 %copy-start.11 = (s32[16,2]{0,1:T(2,128)S(1)}, s32[16,2]{0,1:T(2,128)}, u32[]{:S(2)}) copy-start(s32[16,2]{0,1:T(2,128)} %param.9) | copy-start | bytes 388
  259.4 50.1 %all-to-all-start.2 = ((bf16[64,96,128]{2,1,0:T(8,128)(2,1)}), bf16[64,96,128]{2,1,0:T(8,128)(2,1)}, u32[]{:S(2)}, u32[]{:S(2)}) async-start(bf16[64,96,128]{2,1,0:T(8,128)(2,1)} %reshape.54), calls=%async_computation.3 | async-start | bytes 3145728 | tf_op jit(solution)/shard_map/all_to_all | solution.py:118
  270.4 4.7 %copy-start.3 = (bf16[1,384,4,1024]{1,3,2,0:T(8,128)(2,1)S(1)}, bf16[1,384,4,1024]{1,3,2,0:T(8,128)(2,1)}, u32[]{:S(2)}) copy-start(bf16[1,384,4,1024]{1,3,2,0:T(8,128)(2,1)} %copy-done.2) | copy-start | bytes 9437188
  309.5 68.5 %copy-start.1 = (bf16[1,4096,256]{2,1,0:T(8,128)(2,1)S(1)}, bf16[1,4096,256]{2,1,0:T(8,128)(2,1)}, u32[]{:S(2)}) copy-start(bf16[1,4096,256]{2,1,0:T(8,128)(2,1)} %param.12) | copy-start | bytes 6291460
  314.2 3.6 copy-start.8
  314.2 14.1 %copy-start.9 = (bf16[16,1024]{1,0:T(8,128)(2,1)S(1)}, bf16[16,1024]{1,0:T(8,128)(2,1)}, u32[]{:S(2)}) copy-start(bf16[16,1024]{1,0:T(8,128)(2,1)} %param.7) | copy-start | bytes 98308
  314.2 14.2 %copy-start.10 = (bf16[1024,8]{0,1:T(8,128)(2,1)S(1)}, bf16[1024,8]{0,1:T(8,128)(2,1)}, u32[]{:S(2)}) copy-start(bf16[1024,8]{0,1:T(8,128)(2,1)} %param.10) | copy-start | bytes 49156
Sparse Core Ops, SparseCore 0:
  189.9 61.1 reduce-scatter.1
